TPU v7x, 128 devices: a whole 4x4x4 slice. The times are simulated.
128 devices in a mesh: wide: 16 (over x, z), narrow: 8 (over y, core).
Axes of the slice: x: 4, y: 4, z: 4, core: 2. Of those that a mesh axis runs over, the one named last changes fastest.
Arguments:
- tokens: bfloat16 [16384, 2048], P(('wide', 'narrow')), may hold values from -6 to 6
- queries: bfloat16 [16384, 2048], P(('wide', 'narrow')), may hold values from -5 to 5
- new_kv: bfloat16 [16384, 1024], P(('wide', 'narrow')), may hold values from -5 to 5
- page_pool: bfloat16 [2048, 64, 1024], P('wide', 'narrow'), may hold values from -5 to 5
- seg_ids: int32 [16, 1024], P('wide'), may hold values from 0 to 15, never falling along the last dimension, each value on 1 to 512 neighbouring positions
- cache_len: int32 [16, 16], P('wide'), may hold values from 64 to 512
- page_table: int32 [16, 16, 8], P('wide'), may hold values from 0 to 7, each once within a row
- moves: int32 [16], replicated, may hold values from 0 to 15, as said below
- out_weight: bfloat16 [2048, 2048], replicated, may hold values from -0.125 to 0.125
- norm_gain: float32 [2048], replicated, may hold values from 0.1 to 1.9
- expert_ids: int32 [16384, 6], P(('wide', 'narrow')), may hold values from 0 to 63, all different within a row; in each aligned block of 128 rows (0 to 127, 128 to 255, ...) at most 16 rows name the same one
- gate_weights: float32 [16384, 6], P(('wide', 'narrow')), may hold values from 0.05 to 0.35
- expert_in: bfloat16 [128, 2048, 1408], P(('wide', 'narrow')), may hold values from -0.125 to 0.125
- expert_out: bfloat16 [128, 704, 2048], P(('wide', 'narrow')), may hold values from -0.15625 to 0.15625
Outputs:
- layer_out: bfloat16 [16384, 2048], P(('wide', 'narrow'))
Inputs may be any that keep to these rules, and one draw needn't show every extreme that they name: Slot r of group g holds the request that slot r of group (g - moves[r]) mod 16 held before. No value appears more than 2 times, and some value appears exactly 2 times. The values 1, 15 and 8 each appear. `expert_ids`: within the 128 rows of one device no expert is named more than 16 times; in every draw some device names some expert exactly 16 times. `seg_ids`: never falling along a group's tokens; each of the 16 slots has one token or more. `page_table`: each row is a permutation.
All inputs are finite; a program needn't handle non-finite values.
Results may differ from a plain program's by a relative error of at most 0.006.
Values may be sent and summed in bfloat16 or wider, within the bound.
No kernel may reach another device: no remote copies, remote signals or barrier semaphores. Data moves between devices by JAX's collectives and lax.ppermute only.
A program may use at most 192 MiB of HBM per device.

v0:
```python
import functools

import jax
import jax.numpy as jnp
from jax import lax
from jax.sharding import PartitionSpec as P

QH = 16
KVH = 4
HD = 128
TOPK = 6
PAGE_CAP = 2


norm_eps = 1e-06
block_limit = 512


def rank_among_equal(values):
    length = values.shape[0]
    order = jnp.arange(length, dtype=jnp.int32)
    earlier = (values[None, :] == values[:, None]) & (order[None, :] < order[:, None])
    return jnp.sum(earlier.astype(jnp.int32), axis=1)


def block_scores(q_block, keys):
    return jnp.einsum("bhd,kd->hbk", q_block, keys, preferred_element_type=jnp.float32) * HD ** (
        -0.5
    )


def fresh_scores(start_row, q_heads, key_new, seg_all, block_len):
    q_block = lax.dynamic_slice_in_dim(q_heads, start_row, block_len, 0)
    seg_block = lax.dynamic_slice_in_dim(seg_all, start_row, block_len, 0)
    row_pos = start_row + jnp.arange(block_len, dtype=jnp.int32)
    positions = jnp.arange(seg_all.shape[0], dtype=jnp.int32)
    visible = (seg_block[:, None] == seg_all[None, :]) & (positions[None, :] <= row_pos[:, None])
    scores = jnp.where(visible[None], block_scores(q_block, key_new), -jnp.inf)
    return (q_block, seg_block, scores)


def attend_masked(
    start_row,
    q_heads,
    key_new,
    value_new,
    key_cached,
    value_cached,
    seg_all,
    lengths,
    cache_max,
    block_len,
):
    q_block, seg_block, fresh = fresh_scores(start_row, q_heads, key_new, seg_all, block_len)
    key_req = jnp.arange(key_cached.shape[0], dtype=jnp.int32) // cache_max
    key_pos = jnp.arange(key_cached.shape[0], dtype=jnp.int32) % cache_max
    visible = (seg_block[:, None] == key_req[None, :]) & (
        key_pos[None, :] < lengths[key_req][None, :]
    )
    older = jnp.where(visible[None], block_scores(q_block, key_cached), -jnp.inf)
    row_max = jnp.maximum(jnp.max(fresh, axis=-1), jnp.max(older, axis=-1))
    fresh_exp = jnp.exp(fresh - row_max[..., None])
    older_exp = jnp.exp(older - row_max[..., None])
    row_total = jnp.sum(fresh_exp, axis=-1) + jnp.sum(older_exp, axis=-1)
    fresh_w = (fresh_exp / row_total[..., None]).astype(jnp.bfloat16)
    older_w = (older_exp / row_total[..., None]).astype(jnp.bfloat16)
    attended = jnp.einsum("hbk,kd->bhd", fresh_w, value_new, preferred_element_type=jnp.float32)
    attended = attended + jnp.einsum(
        "hbk,kd->bhd", older_w, value_cached, preferred_element_type=jnp.float32
    )
    return attended.astype(jnp.bfloat16).reshape(block_len, -1)


def expert_apply(rows_in, expert_in, expert_out):
    dims_in = rows_in.shape
    flat = rows_in.reshape(-1, dims_in[-1])
    both = jnp.dot(flat, expert_in[0], preferred_element_type=jnp.float32)
    half_units = both.shape[1] // 2
    hidden = (jax.nn.silu(both[:, :half_units]) * both[:, half_units:]).astype(jnp.bfloat16)
    half_out = jnp.dot(hidden, expert_out[0], preferred_element_type=jnp.float32)
    return half_out.reshape(dims_in)


def shards(
    tokens,
    queries,
    new_kv,
    page_pool,
    seg_ids,
    cache_len,
    page_table,
    moves,
    out_weight,
    norm_gain,
    expert_ids,
    gate_weights,
    expert_in,
    expert_out,
):
    n_wide = lax.axis_size("wide")
    n_narrow = lax.axis_size("narrow")
    my_group = lax.axis_index("wide")
    tok_dev, width = tokens.shape
    group_tok = tok_dev * n_narrow
    requests = moves.shape[0]
    page_rows = page_pool.shape[1]
    kv_feat = page_pool.shape[2]
    pages_each = page_pool.shape[0] // requests
    heads_here = QH // n_narrow
    group_size = QH // KVH
    ranks = rank_among_equal(moves)
    offsets = jnp.arange(n_wide, dtype=jnp.int32)
    places = jnp.arange(PAGE_CAP, dtype=jnp.int32)
    slot_hits = (moves[None, None, :] == offsets[:, None, None]) & (
        ranks[None, None, :] == places[None, :, None]
    )
    picked = jnp.sum(slot_hits.astype(jnp.int32) * jnp.arange(requests, dtype=jnp.int32), axis=2)
    filled = jnp.any(slot_hits, axis=2)
    by_dest = (offsets - my_group) % n_wide
    picked = picked[by_dest]
    filled = filled[by_dest]
    blocks = page_pool.reshape(requests, pages_each * page_rows, kv_feat)
    outgoing = jnp.take(blocks, picked.reshape(-1), axis=0).reshape(
        n_wide, PAGE_CAP, pages_each * page_rows, kv_feat
    )
    outgoing = jnp.where(filled[:, :, None, None], outgoing, jnp.zeros((), outgoing.dtype))
    arrived = lax.all_to_all(outgoing, "wide", split_axis=0, concat_axis=0, tiled=True)
    sources = (my_group - moves) % n_wide
    first_page = (sources * PAGE_CAP + ranks) * pages_each
    page_index = (first_page[:, None] + page_table[0]).reshape(-1)
    arrived = arrived.reshape(n_wide * PAGE_CAP * pages_each, page_rows, kv_feat)
    cached = jnp.take(arrived, page_index, axis=0)
    kv_of_dest = jnp.arange(n_narrow, dtype=jnp.int32) * heads_here // group_size
    q_send = queries.reshape(1, tok_dev, n_narrow, heads_here * HD)
    kv_send = jnp.take(new_kv.reshape(tok_dev, KVH, 2 * HD), kv_of_dest, axis=1).reshape(
        1, tok_dev, n_narrow, 2 * HD
    )
    cache_send = jnp.take(
        cached.reshape(requests * pages_each, page_rows, KVH, 2 * HD), kv_of_dest, axis=2
    )
    q_heads, kv_heads, cache_heads = (
        lax.all_to_all(q_send, "narrow", split_axis=2, concat_axis=1, tiled=True),
        lax.all_to_all(kv_send, "narrow", split_axis=2, concat_axis=1, tiled=True),
        lax.all_to_all(cache_send, "narrow", split_axis=2, concat_axis=1, tiled=True),
    )
    q_heads = q_heads.reshape(group_tok, heads_here, HD)
    kv_heads = kv_heads.reshape(group_tok, 2 * HD)
    cache_max = pages_each * page_rows * n_narrow
    cache_heads = cache_heads.reshape(requests * cache_max, 2 * HD)
    key_new = kv_heads[:, :HD]
    value_new = kv_heads[:, HD:]
    key_cached = cache_heads[:, :HD]
    value_cached = cache_heads[:, HD:]
    seg_all = seg_ids[0]
    lengths = cache_len[0]
    block_len = min(block_limit, group_tok)
    starts = jnp.arange(group_tok // block_len, dtype=jnp.int32) * block_len
    attend_one = functools.partial(
        attend_masked,
        q_heads=q_heads,
        key_new=key_new,
        value_new=value_new,
        key_cached=key_cached,
        value_cached=value_cached,
        seg_all=seg_all,
        lengths=lengths,
        cache_max=cache_max,
        block_len=block_len,
    )
    attended = lax.map(attend_one, starts).reshape(n_narrow, tok_dev, heads_here * HD)
    back_home = lax.all_to_all(attended, "narrow", split_axis=0, concat_axis=2, tiled=True)
    mixed = back_home.reshape(tok_dev, QH * HD)
    residual = tokens.astype(jnp.float32) + jnp.dot(
        mixed, out_weight, preferred_element_type=jnp.float32
    )
    scale_row = lax.rsqrt(jnp.mean(residual * residual, axis=-1, keepdims=True) + norm_eps)
    normed = (residual * scale_row * norm_gain).astype(jnp.bfloat16)
    experts = n_wide * n_narrow // 2
    capacity = tok_dev * TOPK * 4 // (3 * experts)
    flat_ids = expert_ids.reshape(-1)
    onehot = (flat_ids[:, None] == jnp.arange(experts, dtype=jnp.int32)[None, :]).astype(jnp.int32)
    before = jnp.cumsum(onehot, axis=0) - onehot
    slot_place = jnp.sum(before * onehot, axis=1)
    slot_of = flat_ids * capacity + slot_place
    token_of = jnp.arange(tok_dev * TOPK, dtype=jnp.int32) // TOPK
    slot_token = jnp.zeros((experts * capacity,), jnp.int32).at[slot_of].set(token_of)
    slot_used = jnp.zeros((experts * capacity,), jnp.bool_).at[slot_of].set(True)
    outgoing_rows = jnp.where(
        slot_used[:, None], jnp.take(normed, slot_token, axis=0), jnp.zeros((), jnp.bfloat16)
    )
    outgoing_rows = outgoing_rows.reshape(experts, capacity, width)
    outgoing_all = jnp.repeat(outgoing_rows, 2, axis=0)
    half_out = expert_apply(
        lax.all_to_all(outgoing_all, ("wide", "narrow"), split_axis=0, concat_axis=0, tiled=True),
        expert_in,
        expert_out,
    )
    returned = lax.all_to_all(
        half_out.astype(jnp.bfloat16), ("wide", "narrow"), split_axis=0, concat_axis=0, tiled=True
    ).astype(half_out.dtype)
    returned = returned.reshape(experts, 2, capacity, width)
    summed_rows = (returned[:, 0] + returned[:, 1]).astype(jnp.bfloat16)
    summed_rows = summed_rows.reshape(experts * capacity, width)
    picked_rows = jnp.take(summed_rows, slot_of, axis=0)
    weighted = picked_rows.astype(jnp.float32) * gate_weights.reshape(-1)[:, None]
    expert_sum = jnp.sum(weighted.reshape(tok_dev, TOPK, width), axis=1)
    return (residual + expert_sum).astype(jnp.bfloat16)


def solution(mesh):
    placed = (
        P(("wide", "narrow"), None),
        P(("wide", "narrow"), None),
        P(("wide", "narrow"), None),
        P("wide", "narrow", None),
        P("wide", None),
        P("wide", None),
        P("wide", None, None),
        P(),
        P(),
        P(),
        P(("wide", "narrow"), None),
        P(("wide", "narrow"), None),
        P(("wide", "narrow"), None, None),
        P(("wide", "narrow"), None, None),
    )
    return jax.shard_map(
        shards, mesh=mesh, in_specs=placed, out_specs=P(("wide", "narrow"), None), check_vma=False
    )
```

profile of v0, /device:TPU:24, one launch (start us, length us, event | category | flops | bytes accessed | tf_op | source)
XLA Modules:
  0.0 693.2 jit_solution(1184614479564057502)
XLA Ops:
  12.4 8.1 %all-to-all-start.2 = ((bf16[16,2,64,1024]{3,2,1,0:T(8,128)(2,1)}), bf16[16,2,64,1024]{3,2,1,0:T(8,128)(2,1)}, u32[]{:S(2)}, u32[]{:S(2)}) async-start(bf16[16,2,64,1024]{3,2,1,0:T(8,128)(2,1)} %select_select_fusion.1), calls=%async_computation.2 | async-start | bytes 8388608 | tf_op jit(solution)/shard_map/all_to_all | solution.py:127
  26.9 55.5 %all-to-all-done.2 = bf16[16,2,64,1024]{3,2,1,0:T(8,128)(2,1)} async-done(((bf16[16,2,64,1024]{3,2,1,0:T(8,128)(2,1)}), bf16[16,2,64,1024]{3,2,1,0:T(8,128)(2,1)}, u32[]{:S(2)}, u32[]{:S(2)}) %all-to-all-start.2) | async-done | bytes 4194336 | tf_op jit(solution)/shard_map/all_to_all | solution.py:127
  95.3 6.1 all-to-all-start
  133.1 33.4 %all-to-all-done.3 = bf16[128,8,8,256]{3,1,0,2:T(8,128)(2,1)} async-done(((bf16[128,8,8,256]{3,1,0,2:T(8,128)(2,1)}), bf16[128,8,8,256]{3,1,0,2:T(8,128)(2,1)}, u32[]{:S(2)}, u32[]{:S(2)}) %all-to-all-start.3) | async-done | bytes 4194336 | tf_op jit(solution)/shard_map/all_to_all | solution.py:144
  175.6 163.9 %while.12 = (s32[]{:T(128)}, bf16[2,512,256]{2,1,0:T(8,128)(2,1)}, s32[2]{0:T(128)S(1)}, s32[1024]{0:T(1024)S(1)}, s32[1,1024]{1,0:T(1,128)S(1)}, /*index=5*/bf1...) while((s32[]{:T(128)}, bf16[2,512,256]{2,1,0:T(8,128)(2,1)}, ...), condition=%wide.region_8.9_spmd, body=%wide.region_3.8_spmd.sunk | while | flops 4956576256 | bytes 166314976 | solution.py:170
  194.8 16.0 %bitcast_reduce_fusion.5 = (f32[2,512]{1,0:T(2,128)S(1)}, f32[512,2,8192]{2,0,1:T(8,128)}) fusion(pred[512,8192]{1,0:T(8,128)(4,1)} %compare_and_fusion.7, bf16[8192,128]{1,0:T(8,128)(2,1)S(1)} %copy-done.6, bf16[1024,2,128]{0,2,1:T(8,128)(2,1)} %get-tuple-element.400, s32[]{:T(128)S(6)} %select_n.468), kind=kOutput, calls=%fused_computation.11.clone.1 | convolution fusion | flops 2172648448 | bytes 40112132 | tf_op jit(solution)/shard_map/while/body/eval_jaxpr/bhd,kd->hbk/dot_general | solution.py:27
  214.6 15.3 %fusion.88 = f32[2,512]{1,0:T(2,128)S(1)} fusion(f32[512,2,8192]{2,0,1:T(8,128)} %get-tuple-element.366, f32[2,512]{1,0:T(2,128)S(1)} %max.11, pred[512,8192]{1,0:T(8,128)(4,1)S(1)} %copy-done.1), kind=kLoop, calls=%fused_computation.15.clone.1 | loop fusion | flops 33553408 | bytes 37756928 | tf_op jit(solution)/shard_map/while/body/eval_jaxpr/reduce_sum | solution.py:64
  233.4 17.1 %fusion.90 = bf16[2,512,128]{1,2,0:T(8,128)(2,1)S(1)} fusion(f32[2,512,128]{1,2,0:T(8,128)} %fusion.89, bf16[8192,128]{0,1:T(8,128)(2,1)} %get-tuple-element.405, f32[512,2,8192]{2,0,1:T(8,128)} %get-tuple-element.366, f32[2,512]{1,0:T(2,128)S(1)} %add.465, f32[2,512]{1,0:T(2,128)S(1)} %max.11, pred[512,8192]{1,0:T(8,128)(4,1)} %compare_and_fusion.7), kind=kOutput, calls=%fused_computation.31.clone.1 | convolution fusion | flops 2189688832 | bytes 40640512 | tf_op jit(solution)/shard_map/while/body/eval_jaxpr/hbk,kd->bhd/dot_general | solution.py:68
  270.3 16.0 %bitcast_reduce_fusion.5 = (f32[2,512]{1,0:T(2,128)S(1)}, f32[512,2,8192]{2,0,1:T(8,128)}) fusion(pred[512,8192]{1,0:T(8,128)(4,1)} %compare_and_fusion.7, bf16[8192,128]{1,0:T(8,128)(2,1)S(1)} %copy-done.6, bf16[1024,2,128]{0,2,1:T(8,128)(2,1)} %get-tuple-element.400, s32[]{:T(128)S(6)} %select_n.468), kind=kOutput, calls=%fused_computation.11.clone.1 | convolution fusion | flops 2172648448 | bytes 40112132 | tf_op jit(solution)/shard_map/while/body/eval_jaxpr/bhd,kd->hbk/dot_general | solution.py:27
  290.0 15.3 %fusion.88 = f32[2,512]{1,0:T(2,128)S(1)} fusion(f32[512,2,8192]{2,0,1:T(8,128)} %get-tuple-element.366, f32[2,512]{1,0:T(2,128)S(1)} %max.11, pred[512,8192]{1,0:T(8,128)(4,1)S(1)} %copy-done.1), kind=kLoop, calls=%fused_computation.15.clone.1 | loop fusion | flops 33553408 | bytes 37756928 | tf_op jit(solution)/shard_map/while/body/eval_jaxpr/reduce_sum | solution.py:64
  308.8 17.1 %fusion.90 = bf16[2,512,128]{1,2,0:T(8,128)(2,1)S(1)} fusion(f32[2,512,128]{1,2,0:T(8,128)} %fusion.89, bf16[8192,128]{0,1:T(8,128)(2,1)} %get-tuple-element.405, f32[512,2,8192]{2,0,1:T(8,128)} %get-tuple-element.366, f32[2,512]{1,0:T(2,128)S(1)} %add.465, f32[2,512]{1,0:T(2,128)S(1)} %max.11, pred[512,8192]{1,0:T(8,128)(4,1)} %compare_and_fusion.7), kind=kOutput, calls=%fused_computation.31.clone.1 | convolution fusion | flops 2189688832 | bytes 40640512 | tf_op jit(solution)/shard_map/while/body/eval_jaxpr/hbk,kd->bhd/dot_general | solution.py:68
  371.3 6.8 broadcast_in_dim.205
  378.1 110.0 %all_to_all.75 = bf16[128,16,2048]{2,1,0:T(8,128)(2,1)S(1)} all-to-all(bf16[128,16,2048]{2,1,0:T(8,128)(2,1)} %bitcast.221), channel_id=1, replica_groups=mesh['wide'=16,'narrow'=8] {'wide','narrow'}, dimensions={0} | all-to-all | bytes 16777216 | tf_op jit(solution)/shard_map/all_to_all | solution.py:194
  488.1 17.8 %fusion.38 = f32[2048,1408]{0,1:T(8,128)} fusion(bf16[2048,2048]{1,0:T(8,128)(2,1)S(1)} %bitcast.225, bf16[1,2048,1408]{2,1,0:T(8,128)(2,1)} %param.28), kind=kOutput, calls=%fused_computation.84 | convolution fusion | flops 11811160064 | bytes 25690112 | tf_op jit(solution)/shard_map/dot_general | solution.py:77
  505.9 6.4 fusion.37
  516.8 11.4 %convolution_convert_fusion = bf16[128,16,2048]{2,0,1:T(8,128)(2,1)} fusion(bf16[128,16,704]{2,1,0:T(8,128)(2,1)} %bitcast.232, bf16[1,704,2048]{2,1,0:T(8,128)(2,1)S(1)} %copy-done), kind=kOutput, calls=%fused_computation.86 | convolution fusion | flops 5909774336 | bytes 14155776 | tf_op jit(solution)/shard_map/dot_general | solution.py:80
  528.2 11.2 %copy.130 = bf16[128,16,2048]{2,1,0:T(8,128)(2,1)} copy(bf16[128,16,2048]{2,0,1:T(8,128)(2,1)} %convolution_convert_fusion) | data formatting | bytes 16777216 | tf_op jit(solution)/shard_map/convert_element_type | solution.py:199
  539.5 9.3 %all-to-all-start.6 = ((bf16[128,16,2048]{2,1,0:T(8,128)(2,1)}), bf16[128,16,2048]{2,1,0:T(8,128)(2,1)}, u32[]{:S(2)}, u32[]{:S(2)}) async-start(bf16[128,16,2048]{2,1,0:T(8,128)(2,1)} %copy.130), calls=%async_computation.6 | async-start | bytes 16777216 | tf_op jit(solution)/shard_map/all_to_all | solution.py:198
  549.3 100.6 %all-to-all-done.6 = bf16[128,16,2048]{2,1,0:T(8,128)(2,1)} async-done(((bf16[128,16,2048]{2,1,0:T(8,128)(2,1)}), bf16[128,16,2048]{2,1,0:T(8,128)(2,1)}, u32[]{:S(2)}, u32[]{:S(2)}) %all-to-all-start.6) | async-done | bytes 8388640 | tf_op jit(solution)/shard_map/all_to_all | solution.py:198
  650.0 11.2 %convert.1 = f32[64,2,16,2048]{3,2,1,0:T(8,128)} convert(bf16[64,2,16,2048]{3,2,1,0:T(8,128)(2,1)} %bitcast.66) | non-fusion elementwise | flops 4194304 | bytes 25165824 | tf_op jit(solution)/shard_map/reshape | solution.py:201
  661.2 8.5 %fusion.36 = bf16[64,1,16,2048]{3,2,0,1:T(8,128)(2,1)} fusion(f32[64,2,16,2048]{3,2,1,0:T(8,128)} %convert.1), kind=kLoop, calls=%fused_computation.79 | loop fusion | flops 4194304 | bytes 20971520 | tf_op jit(solution)/shard_map/convert_element_type | solution.py:202
  669.7 9.9 %gather_fusion.7 = bf16[768,2048]{1,0:T(8,128)(2,1)} fusion(bf16[1024,2048]{1,0:T(8,128)(2,1)} %bitcast.220, s32[1024]{0:T(1024)S(1)} %pad_clamp_fusion), kind=kCustom, calls=%fused_computation.7 | custom fusion | bytes 6294528 | tf_op jit(solution)/shard_map/jit(_take)/gather | solution.py:204
  679.6 6.3 gather.58
  685.8 6.1 multiply_reduce_fusion
  (182 shorter events, 160.2 us)
Async XLA Ops:
  0.0 516.8 %copy-start = (bf16[1,704,2048]{2,1,0:T(8,128)(2,1)S(1)}, bf16[1,704,2048]{2,1,0:T(8,128)(2,1)}, u32[]{:S(2)}) copy-start(bf16[1,704,2048]{2,1,0:T(8,128)(2,1)} %param.29) | copy-start | bytes 8650756
  12.4 8.1 %copy-start.18 = (s32[16]{0:T(128)S(1)}, s32[16]{0:T(128)}, u32[]{:S(2)}) copy-start(s32[16]{0:T(128)} %param.23) | copy-start | bytes 196
  12.4 8.4 %copy-start.16 = (s32[1,16,8]{1,2,0:T(8,128)S(1)}, s32[1,16,8]{1,2,0:T(8,128)}, u32[]{:S(2)}) copy-start(s32[1,16,8]{1,2,0:T(8,128)} %param.22) | copy-start | bytes 1540
  12.4 8.6 %copy-start.7 = (bf16[128,1024]{1,0:T(8,128)(2,1)S(1)}, bf16[128,1024]{1,0:T(8,128)(2,1)}, u32[]{:S(2)}) copy-start(bf16[128,1024]{1,0:T(8,128)(2,1)} %param.18) | copy-start | bytes 786436
  12.4 69.9 %all-to-all-start.2 = ((bf16[16,2,64,1024]{3,2,1,0:T(8,128)(2,1)}), bf16[16,2,64,1024]{3,2,1,0:T(8,128)(2,1)}, u32[]{:S(2)}, u32[]{:S(2)}) async-start(bf16[16,2,64,1024]{3,2,1,0:T(8,128)(2,1)} %select_select_fusion.1), calls=%async_computation.2 | async-start | bytes 8388608 | tf_op jit(solution)/shard_map/all_to_all | solution.py:127
  82.3 12.9 %all-to-all-start.1 = ((bf16[1,128,8,256]{3,1,0,2:T(8,128)(2,1)}), bf16[1,128,8,256]{3,1,0,2:T(8,128)(2,1)S(1)}, u32[]{:S(2)}, u32[]{:S(2)}) async-start(bf16[1,128,8,256]{3,1,0,2:T(8,128)(2,1)} %fusion.42), calls=%async_computation.1 | async-start | bytes 1048576 | tf_op jit(solution)/shard_map/all_to_all | solution.py:143
  95.3 18.6 %all-to-all-start = ((bf16[1,128,8,256]{1,3,0,2:T(8,128)(2,1)}), bf16[1,128,8,256]{1,3,0,2:T(8,128)(2,1)}, u32[]{:S(2)}, u32[]{:S(2)}) async-start(bf16[1,128,8,256]{1,3,0,2:T(8,128)(2,1)} %bitcast.234), calls=%async_computation | async-start | bytes 1048576 | tf_op jit(solution)/shard_map/all_to_all | solution.py:142
  113.9 4.9 copy-start.10
  113.9 52.6 %all-to-all-start.3 = ((bf16[128,8,8,256]{3,1,0,2:T(8,128)(2,1)}), bf16[128,8,8,256]{3,1,0,2:T(8,128)(2,1)}, u32[]{:S(2)}, u32[]{:S(2)}) async-start(bf16[128,8,8,256]{3,1,0,2:T(8,128)(2,1)} %select_bitcast_fusion), calls=%async_computation.3 | async-start | bytes 8388608 | tf_op jit(solution)/shard_map/all_to_all | solution.py:144
  171.5 4.1 copy-start.4
  171.5 4.1 copy-start.9
  175.6 169.4 %copy-start.14 = (s32[768]{0:T(1024)S(1)}, s32[768]{0:T(1024)}, u32[]{:S(2)}) copy-start(s32[768]{0:T(1024)} %fusion.53) | copy-start | bytes 9220
  189.7 5.1 copy-start.6
  210.8 3.8 copy-start.1
  265.2 5.1 copy-start.6
  286.3 3.7 copy-start.1
  305.3 1.2 copy-start.8
  339.5 13.7 %all-to-all-start.4 = ((bf16[8,128,256]{2,1,0:T(8,128)(2,1)}), bf16[8,128,256]{2,1,0:T(8,128)(2,1)S(1)}, u32[]{:S(2)}, u32[]{:S(2)}) async-start(bf16[8,128,256]{2,1,0:T(8,128)(2,1)} %bitcast.237), calls=%async_computation.4 | async-start | bytes 1048576 | tf_op jit(solution)/shard_map/all_to_all | solution.py:171
  355.3 5.9 copy-start.15
  539.5 9.3 %copy-start.13 = (s32[768]{0:T(1024)S(1)}, s32[768]{0:T(1024)}, u32[]{:S(2)}) copy-start(s32[768]{0:T(1024)} %copy-done.12) | copy-start | bytes 9220
  539.5 9.5 %copy-start.11 = (s32[128,6]{0,1:T(8,128)S(1)}, s32[128,6]{0,1:T(8,128)}, u32[]{:S(2)}) copy-start(s32[128,6]{0,1:T(8,128)} %param.26) | copy-start | bytes 9220
  539.5 9.7 %copy-start.17 = (f32[128,6]{0,1:T(8,128)S(1)}, f32[128,6]{0,1:T(8,128)}, u32[]{:S(2)}) copy-start(f32[128,6]{0,1:T(8,128)} %param.27) | copy-start | bytes 9220
  539.5 110.5 %all-to-all-start.6 = ((bf16[128,16,2048]{2,1,0:T(8,128)(2,1)}), bf16[128,16,2048]{2,1,0:T(8,128)(2,1)}, u32[]{:S(2)}, u32[]{:S(2)}) async-start(bf16[128,16,2048]{2,1,0:T(8,128)(2,1)} %copy.130), calls=%async_computation.6 | async-start | bytes 16777216 | tf_op jit(solution)/shard_map/all_to_all | solution.py:198
  685.8 6.1 copy-start.3
  (4 other events, 3.6 us)
where the time goes:
time: 707 us; the launch traced here: 693 us
  waiting for transfers between devices  195 us (28%)
  other arithmetic  127 us (18%)
  matrix products  110 us (16%)
  blocking collectives  110 us (16%)
  local copies, waits for them, and re-layouts  95.3 us (13%)
  starting transfers between devices  38.6 us (5%)
  loops' own time  16.9 us (2%)
    all_to_all x1, blocking collectives, shards(): lax.all_to_all(outgoing_all, ('wide', 'narrow'), split_axis=0, concat_axi...  110 us
    all_to_all x1, waiting for transfers between devices, shards(): lax.all_to_all(half_out.astype(jnp.bfloat16), ('wide', 'narrow'), split_a...  101 us
    all_to_all x1, waiting for transfers between devices, shards(): lax.all_to_all(outgoing, 'wide', split_axis=0, concat_axis=0, tiled=True)  55.5 us
    dot_general x4, matrix products, block_scores(): jnp.einsum('bhd,kd->hbk', q_block, keys, preferred_element_type=jnp.float32)  36.7 us
    dot_general x2, matrix products, attend_masked(): jnp.einsum('hbk,kd->bhd', older_w, value_cached, preferred_element_type=j...  34.3 us
    all_to_all x1, waiting for transfers between devices, shards(): lax.all_to_all(cache_send, 'narrow', split_axis=2, concat_axis=1, tiled=T...  33.4 us
    reduce_sum x4, other arithmetic, attend_masked(): row_total = jnp.sum(fresh_exp, axis=-1) + jnp.sum(older_exp, axis=-1)  32.9 us
    dot_general x1, matrix products, expert_apply(): both = jnp.dot(flat, expert_in[0], preferred_element_type=jnp.float32)  17.8 us
  transfers between devices with their start and end apart: 6, of which 5 were waited for; matrix products, arithmetic and copies ran while one was open for 6% of the time, Pallas kernels for 0%

commit v1 on v0

--- a/solution.py
+++ b/solution.py
@@ -3,6 +3,7 @@
 import jax
 import jax.numpy as jnp
 from jax import lax
+from jax.sharding import Mesh
 from jax.sharding import PartitionSpec as P
 
 QH = 16
@@ -10,6 +11,9 @@
 HD = 128
 TOPK = 6
 PAGE_CAP = 2
+NARROW = ("y", "core")
+CHIPS = ("wide", "y")
+WN = ("wide", "y", "core")
 
 
 norm_eps = 1e-06
@@ -98,7 +102,7 @@
     expert_out,
 ):
     n_wide = lax.axis_size("wide")
-    n_narrow = lax.axis_size("narrow")
+    n_narrow = lax.axis_size("y") * lax.axis_size("core")
     my_group = lax.axis_index("wide")
     tok_dev, width = tokens.shape
     group_tok = tok_dev * n_narrow
@@ -139,9 +143,9 @@
         cached.reshape(requests * pages_each, page_rows, KVH, 2 * HD), kv_of_dest, axis=2
     )
     q_heads, kv_heads, cache_heads = (
-        lax.all_to_all(q_send, "narrow", split_axis=2, concat_axis=1, tiled=True),
-        lax.all_to_all(kv_send, "narrow", split_axis=2, concat_axis=1, tiled=True),
-        lax.all_to_all(cache_send, "narrow", split_axis=2, concat_axis=1, tiled=True),
+        lax.all_to_all(q_send, NARROW, split_axis=2, concat_axis=1, tiled=True),
+        lax.all_to_all(kv_send, NARROW, split_axis=2, concat_axis=1, tiled=True),
+        lax.all_to_all(cache_send, NARROW, split_axis=2, concat_axis=1, tiled=True),
     )
     q_heads = q_heads.reshape(group_tok, heads_here, HD)
     kv_heads = kv_heads.reshape(group_tok, 2 * HD)
@@ -168,7 +172,7 @@
         block_len=block_len,
     )
     attended = lax.map(attend_one, starts).reshape(n_narrow, tok_dev, heads_here * HD)
-    back_home = lax.all_to_all(attended, "narrow", split_axis=0, concat_axis=2, tiled=True)
+    back_home = lax.all_to_all(attended, NARROW, split_axis=0, concat_axis=2, tiled=True)
     mixed = back_home.reshape(tok_dev, QH * HD)
     residual = tokens.astype(jnp.float32) + jnp.dot(
         mixed, out_weight, preferred_element_type=jnp.float32
@@ -189,18 +193,16 @@
         slot_used[:, None], jnp.take(normed, slot_token, axis=0), jnp.zeros((), jnp.bfloat16)
     )
     outgoing_rows = outgoing_rows.reshape(experts, capacity, width)
-    outgoing_all = jnp.repeat(outgoing_rows, 2, axis=0)
-    half_out = expert_apply(
-        lax.all_to_all(outgoing_all, ("wide", "narrow"), split_axis=0, concat_axis=0, tiled=True),
-        expert_in,
-        expert_out,
-    )
-    returned = lax.all_to_all(
-        half_out.astype(jnp.bfloat16), ("wide", "narrow"), split_axis=0, concat_axis=0, tiled=True
-    ).astype(half_out.dtype)
-    returned = returned.reshape(experts, 2, capacity, width)
-    summed_rows = (returned[:, 0] + returned[:, 1]).astype(jnp.bfloat16)
-    summed_rows = summed_rows.reshape(experts * capacity, width)
+    at_chip = lax.all_to_all(outgoing_rows, CHIPS, split_axis=0, concat_axis=0, tiled=True)
+    both_cores = lax.all_gather(at_chip, "core", axis=0, tiled=False)
+    half_out = expert_apply(both_cores, expert_in, expert_out)
+    core = lax.axis_index("core")
+    mine = lax.dynamic_index_in_dim(half_out, core, 0, keepdims=False)
+    theirs = lax.dynamic_index_in_dim(half_out, 1 - core, 0, keepdims=False)
+    partner = lax.ppermute(theirs, "core", perm=[(0, 1), (1, 0)])
+    summed = (mine + partner).astype(jnp.bfloat16)
+    returned = lax.all_to_all(summed, CHIPS, split_axis=0, concat_axis=0, tiled=True)
+    summed_rows = returned.reshape(experts * capacity, width)
     picked_rows = jnp.take(summed_rows, slot_of, axis=0)
     weighted = picked_rows.astype(jnp.float32) * gate_weights.reshape(-1)[:, None]
     expert_sum = jnp.sum(weighted.reshape(tok_dev, TOPK, width), axis=1)
@@ -209,21 +211,22 @@
 
 def solution(mesh):
     placed = (
-        P(("wide", "narrow"), None),
-        P(("wide", "narrow"), None),
-        P(("wide", "narrow"), None),
-        P("wide", "narrow", None),
+        P(WN, None),
+        P(WN, None),
+        P(WN, None),
+        P("wide", NARROW, None),
         P("wide", None),
         P("wide", None),
         P("wide", None, None),
         P(),
         P(),
         P(),
-        P(("wide", "narrow"), None),
-        P(("wide", "narrow"), None),
-        P(("wide", "narrow"), None, None),
-        P(("wide", "narrow"), None, None),
-    )
+        P(WN, None),
+        P(WN, None),
+        P(WN, None, None),
+        P(WN, None, None),
+    )
+    mesh = Mesh(mesh.devices.reshape(mesh.shape["wide"], -1, 2), ("wide", "y", "core"))
     return jax.shard_map(
-        shards, mesh=mesh, in_specs=placed, out_specs=P(("wide", "narrow"), None), check_vma=False
-    )
+        shards, mesh=mesh, in_specs=placed, out_specs=P(WN, None), check_vma=False
+    )

time: 707 us -> 637 us (0.901)
  blocking collectives: 110 us -> 64.6 us
  between operations: 0.74 us -> 14.2 us
  other arithmetic: 127 us -> 115 us
  waiting for transfers between devices: 195 us -> 185 us
  local copies, waits for them, and re-layouts: 95.3 us -> 85.6 us
    all_to_all x1, blocking collectives: 110 us -> 64.6 us  [shards(): lax.all_to_all(outgoing_rows, CHIPS, split_axis=0, concat_axis=0, tiled=T...]
    all_to_all x5, waiting for transfers between devices: 139 us -> 95 us  [the longest x1 56.3 us: shards(): lax.all_to_all(summed, CHIPS, split_axis=0, concat_axis=0, tiled=True)]
    all_gather x0 -> x1, waiting for transfers between devices: none -> 21.8 us  [shards(): both_cores = lax.all_gather(at_chip, 'core', axis=0, tiled=False)]
    ppermute x0 -> x1, waiting for transfers between devices: none -> 13.2 us  [shards(): partner = lax.ppermute(theirs, 'core', perm=[(0, 1), (1, 0)])]
    convert_element_type x1 -> x0, local copies, waits for them, and re-layouts: 11.2 us -> none  [shards(): half_out.astype(jnp.bfloat16)]
    reshape x1 -> x0, other arithmetic: 11.2 us -> none  [shards(): returned = returned.reshape(experts, 2, capacity, width)]
  transfers between devices with their start and end apart: 6 -> 8, of which waited for: 5 -> 7; matrix products, arithmetic and copies ran while one was open for 6% -> 7% of each run, Pallas kernels for 0% -> 0%
where the time goes in v1:
time: 637 us; the launch traced here: 629 us
  waiting for transfers between devices  185 us (29%)
  other arithmetic  115 us (18%)
  matrix products  108 us (17%)
  local copies, waits for them, and re-layouts  85.6 us (13%)
  blocking collectives  64.6 us (10%)
  starting transfers between devices  40.7 us (6%)
  loops' own time  14.7 us (2%)
  between operations  14.2 us (2%)
    all_to_all x1, blocking collectives, shards(): lax.all_to_all(outgoing_rows, CHIPS, split_axis=0, concat_axis=0, tiled=T...  64.6 us
    all_to_all x1, waiting for transfers between devices, shards(): lax.all_to_all(summed, CHIPS, split_axis=0, concat_axis=0, tiled=True)  56.3 us
    all_to_all x1, waiting for transfers between devices, shards(): lax.all_to_all(outgoing, 'wide', split_axis=0, concat_axis=0, tiled=True)  55.5 us
    dot_general x4, matrix products, block_scores(): jnp.einsum('bhd,kd->hbk', q_block, keys, preferred_element_type=jnp.float32)  36.7 us
    dot_general x2, matrix products, attend_masked(): jnp.einsum('hbk,kd->bhd', older_w, value_cached, preferred_element_type=j...  34.3 us
    all_to_all x1, waiting for transfers between devices, shards(): lax.all_to_all(cache_send, NARROW, split_axis=2, concat_axis=1, tiled=True)  33.4 us
    reduce_sum x4, other arithmetic, attend_masked(): row_total = jnp.sum(fresh_exp, axis=-1) + jnp.sum(older_exp, axis=-1)  32.9 us
    all_gather x1, waiting for transfers between devices, shards(): both_cores = lax.all_gather(at_chip, 'core', axis=0, tiled=False)  21.8 us
  transfers between devices with their start and end apart: 8, of which 7 were waited for; matrix products, arithmetic and copies ran while one was open for 7% of the time, Pallas kernels for 0%

profile of v1, /device:TPU:24, one launch (start us, length us, event | category | flops | bytes accessed | tf_op | source)
XLA Modules:
  0.0 628.6 jit_solution(13159696289208965019)
XLA Ops:
  19.0 8.1 %all-to-all-start.2 = ((bf16[16,2,64,1024]{3,2,1,0:T(8,128)(2,1)}), bf16[16,2,64,1024]{3,2,1,0:T(8,128)(2,1)}, u32[]{:S(2)}, u32[]{:S(2)}) async-start(bf16[16,2,64,1024]{3,2,1,0:T(8,128)(2,1)} %select_select_fusion.1), calls=%async_computation.2 | async-start | bytes 8388608 | tf_op jit(solution)/shard_map/all_to_all | solution.py:131
  33.4 55.5 %all-to-all-done.2 = bf16[16,2,64,1024]{3,2,1,0:T(8,128)(2,1)} async-done(((bf16[16,2,64,1024]{3,2,1,0:T(8,128)(2,1)}), bf16[16,2,64,1024]{3,2,1,0:T(8,128)(2,1)}, u32[]{:S(2)}, u32[]{:S(2)}) %all-to-all-start.2) | async-done | bytes 4194336 | tf_op jit(solution)/shard_map/all_to_all | solution.py:131
  101.8 6.1 all-to-all-start
  139.6 33.4 %all-to-all-done.3 = bf16[128,8,8,256]{3,1,0,2:T(8,128)(2,1)} async-done(((bf16[128,8,8,256]{3,1,0,2:T(8,128)(2,1)}), bf16[128,8,8,256]{3,1,0,2:T(8,128)(2,1)}, u32[]{:S(2)}, u32[]{:S(2)}) %all-to-all-start.3) | async-done | bytes 4194336 | tf_op jit(solution)/shard_map/all_to_all | solution.py:148
  182.2 161.7 %while.12 = (s32[]{:T(128)}, bf16[2,512,256]{2,1,0:T(8,128)(2,1)}, s32[2]{0:T(128)S(1)}, s32[1024]{0:T(1024)S(1)}, s32[1,1024]{1,0:T(1,128)S(1)}, /*index=5*/bf1...) while((s32[]{:T(128)}, bf16[2,512,256]{2,1,0:T(8,128)(2,1)}, ...), condition=%wide.region_8.9_spmd, body=%wide.region_3.8_spmd.sunk | while | flops 4956576256 | bytes 166314976 | solution.py:174
  201.3 16.0 %bitcast_reduce_fusion.5 = (f32[2,512]{1,0:T(2,128)S(1)}, f32[512,2,8192]{2,0,1:T(8,128)}) fusion(pred[512,8192]{1,0:T(8,128)(4,1)} %compare_and_fusion.7, bf16[8192,128]{1,0:T(8,128)(2,1)S(1)} %copy-done.7, bf16[1024,2,128]{0,2,1:T(8,128)(2,1)} %get-tuple-element.400, s32[]{:T(128)S(6)} %select_n.477), kind=kOutput, calls=%fused_computation.11.clone.1 | convolution fusion | flops 2172648448 | bytes 40112132 | tf_op jit(solution)/shard_map/while/body/eval_jaxpr/bhd,kd->hbk/dot_general | solution.py:31
  221.1 15.3 %fusion.88 = f32[2,512]{1,0:T(2,128)S(1)} fusion(f32[512,2,8192]{2,0,1:T(8,128)} %get-tuple-element.366, f32[2,512]{1,0:T(2,128)S(1)} %max.11, pred[512,8192]{1,0:T(8,128)(4,1)S(1)} %copy-done.1), kind=kLoop, calls=%fused_computation.15.clone.1 | loop fusion | flops 33553408 | bytes 37756928 | tf_op jit(solution)/shard_map/while/body/eval_jaxpr/reduce_sum | solution.py:68
  239.9 17.1 %fusion.90 = bf16[2,512,128]{1,2,0:T(8,128)(2,1)S(1)} fusion(f32[2,512,128]{1,2,0:T(8,128)} %fusion.89, bf16[8192,128]{0,1:T(8,128)(2,1)} %get-tuple-element.405, f32[512,2,8192]{2,0,1:T(8,128)} %get-tuple-element.366, f32[2,512]{1,0:T(2,128)S(1)} %add.473, f32[2,512]{1,0:T(2,128)S(1)} %max.11, pred[512,8192]{1,0:T(8,128)(4,1)} %compare_and_fusion.7), kind=kOutput, calls=%fused_computation.31.clone.1 | convolution fusion | flops 2189688832 | bytes 40640512 | tf_op jit(solution)/shard_map/while/body/eval_jaxpr/hbk,kd->bhd/dot_general | solution.py:72
  276.8 16.0 %bitcast_reduce_fusion.5 = (f32[2,512]{1,0:T(2,128)S(1)}, f32[512,2,8192]{2,0,1:T(8,128)}) fusion(pred[512,8192]{1,0:T(8,128)(4,1)} %compare_and_fusion.7, bf16[8192,128]{1,0:T(8,128)(2,1)S(1)} %copy-done.7, bf16[1024,2,128]{0,2,1:T(8,128)(2,1)} %get-tuple-element.400, s32[]{:T(128)S(6)} %select_n.477), kind=kOutput, calls=%fused_computation.11.clone.1 | convolution fusion | flops 2172648448 | bytes 40112132 | tf_op jit(solution)/shard_map/while/body/eval_jaxpr/bhd,kd->hbk/dot_general | solution.py:31
  296.6 15.3 %fusion.88 = f32[2,512]{1,0:T(2,128)S(1)} fusion(f32[512,2,8192]{2,0,1:T(8,128)} %get-tuple-element.366, f32[2,512]{1,0:T(2,128)S(1)} %max.11, pred[512,8192]{1,0:T(8,128)(4,1)S(1)} %copy-done.1), kind=kLoop, calls=%fused_computation.15.clone.1 | loop fusion | flops 33553408 | bytes 37756928 | tf_op jit(solution)/shard_map/while/body/eval_jaxpr/reduce_sum | solution.py:68
  315.3 17.1 %fusion.90 = bf16[2,512,128]{1,2,0:T(8,128)(2,1)S(1)} fusion(f32[2,512,128]{1,2,0:T(8,128)} %fusion.89, bf16[8192,128]{0,1:T(8,128)(2,1)} %get-tuple-element.405, f32[512,2,8192]{2,0,1:T(8,128)} %get-tuple-element.366, f32[2,512]{1,0:T(2,128)S(1)} %add.473, f32[2,512]{1,0:T(2,128)S(1)} %max.11, pred[512,8192]{1,0:T(8,128)(4,1)} %compare_and_fusion.7), kind=kOutput, calls=%fused_computation.31.clone.1 | convolution fusion | flops 2189688832 | bytes 40640512 | tf_op jit(solution)/shard_map/while/body/eval_jaxpr/hbk,kd->bhd/dot_general | solution.py:72
  365.7 6.0 gather_fusion.6
  374.3 64.6 %all_to_all.75 = bf16[64,16,2048]{2,1,0:T(8,128)(2,1)} all-to-all(bf16[64,16,2048]{2,1,0:T(8,128)(2,1)S(1)} %select_select_fusion), channel_id=1, replica_groups=mesh['wide'=16,'y'=4,'core'=2] {'wide','y'}, dimensions={0} | all-to-all | bytes 8388608 | tf_op jit(solution)/shard_map/all_to_all | solution.py:196
  438.9 21.8 %all-gather.3.cloned.1.call-done = bf16[128,16,2048]{2,1,0:T(8,128)(2,1)} async-done(((bf16[64,16,2048]{2,1,0:T(8,128)(2,1)}), bf16[128,16,2048]{2,1,0:T(8,128)(2,1)}) %all-gather.3.cloned.1.call-update) | async-done | bytes 8388624 | tf_op jit(solution)/shard_map/all_gather | solution.py:197
  460.7 18.8 %fusion.37 = f32[2048,1408]{0,1:T(8,128)} fusion(bf16[2048,2048]{1,0:T(8,128)(2,1)} %bitcast.237, bf16[1,2048,1408]{2,1,0:T(8,128)(2,1)} %param.28), kind=kOutput, calls=%fused_computation.83 | convolution fusion | flops 11811160064 | bytes 25690112 | tf_op jit(solution)/shard_map/dot_general | solution.py:81
  479.5 6.4 %fusion.36 = bf16[2048,704]{0,1:T(8,128)(2,1)} fusion(f32[2048,1408]{0,1:T(8,128)} %fusion.37), kind=kLoop, calls=%fused_computation.82 | loop fusion | flops 8650752 | bytes 14417920 | tf_op jit(solution)/shard_map/convert_element_type | solution.py:83
  490.6 8.7 %fusion.39 = f32[2,64,16,2048]{3,2,1,0:T(8,128)S(1)} fusion(bf16[2,64,16,704]{3,2,1,0:T(8,128)(2,1)} %bitcast.226, bf16[1,704,2048]{2,1,0:T(8,128)(2,1)S(1)} %copy-done), kind=kOutput, calls=%fused_computation.88 | convolution fusion | flops 5905580032 | bytes 22544384 | tf_op jit(solution)/shard_map/dot_general | solution.py:84
  507.8 13.2 %collective-permute-done = f32[64,16,2048]{2,1,0:T(8,128)} collective-permute-done((f32[64,16,2048]{2,1,0:T(8,128)}, f32[64,16,2048]{2,1,0:T(8,128)}, u32[]{:S(2)}, u32[]{:S(2)}) %collective-permute-start) | collective-permute-done | bytes 8388640 | tf_op jit(solution)/shard_map/ppermute | solution.py:202
  521.0 9.2 %fusion.35 = bf16[64,16,2048]{2,1,0:T(8,128)(2,1)} fusion(f32[64,16,2048]{2,1,0:T(8,128)} %collective-permute-done, f32[2,64,16,2048]{3,2,1,0:T(8,128)} %copy-done.2, s32[]{:T(128)S(6)} %select_n.283), kind=kLoop, calls=%fused_computation.78 | loop fusion | flops 4194304 | bytes 20971524 | tf_op jit(solution)/shard_map/convert_element_type | solution.py:203
  530.2 11.1 %all-to-all-start.6 = ((bf16[64,16,2048]{2,1,0:T(8,128)(2,1)}), bf16[64,16,2048]{2,1,0:T(8,128)(2,1)}, u32[]{:S(2)}, u32[]{:S(2)}) async-start(bf16[64,16,2048]{2,1,0:T(8,128)(2,1)} %fusion.35), calls=%async_computation.6 | async-start | bytes 8388608 | tf_op jit(solution)/shard_map/all_to_all | solution.py:204
  541.8 56.3 %all-to-all-done.6 = bf16[64,16,2048]{2,1,0:T(8,128)(2,1)} async-done(((bf16[64,16,2048]{2,1,0:T(8,128)(2,1)}), bf16[64,16,2048]{2,1,0:T(8,128)(2,1)}, u32[]{:S(2)}, u32[]{:S(2)}) %all-to-all-start.6) | async-done | bytes 4194336 | tf_op jit(solution)/shard_map/all_to_all | solution.py:204
  598.2 9.9 %gather_fusion.7 = bf16[768,2048]{1,0:T(8,128)(2,1)} fusion(bf16[1024,2048]{1,0:T(8,128)(2,1)} %bitcast.67, s32[1024]{0:T(1024)S(1)} %pad_clamp_fusion), kind=kCustom, calls=%fused_computation.7 | custom fusion | bytes 6294528 | tf_op jit(solution)/shard_map/jit(_take)/gather | solution.py:206
  608.0 6.3 gather.58
  614.3 6.1 multiply_reduce_fusion
  (187 shorter events, 161.5 us)
Async XLA Ops:
  6.5 484.1 %copy-start = (bf16[1,704,2048]{2,1,0:T(8,128)(2,1)S(1)}, bf16[1,704,2048]{2,1,0:T(8,128)(2,1)}, u32[]{:S(2)}) copy-start(bf16[1,704,2048]{2,1,0:T(8,128)(2,1)} %param.29) | copy-start | bytes 8650756
  18.9 8.1 %copy-start.19 = (s32[16]{0:T(128)S(1)}, s32[16]{0:T(128)}, u32[]{:S(2)}) copy-start(s32[16]{0:T(128)} %param.23) | copy-start | bytes 196
  18.9 8.4 %copy-start.17 = (s32[1,16,8]{1,2,0:T(8,128)S(1)}, s32[1,16,8]{1,2,0:T(8,128)}, u32[]{:S(2)}) copy-start(s32[1,16,8]{1,2,0:T(8,128)} %param.22) | copy-start | bytes 1540
  19.0 8.6 %copy-start.8 = (bf16[128,1024]{1,0:T(8,128)(2,1)S(1)}, bf16[128,1024]{1,0:T(8,128)(2,1)}, u32[]{:S(2)}) copy-start(bf16[128,1024]{1,0:T(8,128)(2,1)} %param.18) | copy-start | bytes 786436
  19.0 69.9 %all-to-all-start.2 = ((bf16[16,2,64,1024]{3,2,1,0:T(8,128)(2,1)}), bf16[16,2,64,1024]{3,2,1,0:T(8,128)(2,1)}, u32[]{:S(2)}, u32[]{:S(2)}) async-start(bf16[16,2,64,1024]{3,2,1,0:T(8,128)(2,1)} %select_select_fusion.1), calls=%async_computation.2 | async-start | bytes 8388608 | tf_op jit(solution)/shard_map/all_to_all | solution.py:131
  88.9 12.9 %all-to-all-start.1 = ((bf16[1,128,8,256]{3,1,0,2:T(8,128)(2,1)}), bf16[1,128,8,256]{3,1,0,2:T(8,128)(2,1)S(1)}, u32[]{:S(2)}, u32[]{:S(2)}) async-start(bf16[1,128,8,256]{3,1,0,2:T(8,128)(2,1)} %fusion.41), calls=%async_computation.1 | async-start | bytes 1048576 | tf_op jit(solution)/shard_map/all_to_all | solution.py:147
  101.8 18.6 %all-to-all-start = ((bf16[1,128,8,256]{1,3,0,2:T(8,128)(2,1)}), bf16[1,128,8,256]{1,3,0,2:T(8,128)(2,1)}, u32[]{:S(2)}, u32[]{:S(2)}) async-start(bf16[1,128,8,256]{1,3,0,2:T(8,128)(2,1)} %bitcast.228), calls=%async_computation | async-start | bytes 1048576 | tf_op jit(solution)/shard_map/all_to_all | solution.py:146
  120.4 4.9 copy-start.11
  120.4 52.6 %all-to-all-start.3 = ((bf16[128,8,8,256]{3,1,0,2:T(8,128)(2,1)}), bf16[128,8,8,256]{3,1,0,2:T(8,128)(2,1)}, u32[]{:S(2)}, u32[]{:S(2)}) async-start(bf16[128,8,8,256]{3,1,0,2:T(8,128)(2,1)} %select_bitcast_fusion), calls=%async_computation.3 | async-start | bytes 8388608 | tf_op jit(solution)/shard_map/all_to_all | solution.py:148
  178.0 4.1 copy-start.5
  178.0 4.1 copy-start.10
  182.2 167.2 %copy-start.15 = (s32[768]{0:T(1024)S(1)}, s32[768]{0:T(1024)}, u32[]{:S(2)}) copy-start(s32[768]{0:T(1024)} %fusion.52) | copy-start | bytes 9220
  196.3 5.1 copy-start.7
  271.7 5.1 copy-start.7
  343.8 13.8 %all-to-all-start.4 = ((bf16[8,128,256]{2,1,0:T(8,128)(2,1)}), bf16[8,128,256]{2,1,0:T(8,128)(2,1)S(1)}, u32[]{:S(2)}, u32[]{:S(2)}) async-start(bf16[8,128,256]{2,1,0:T(8,128)(2,1)} %bitcast.231), calls=%async_computation.4 | async-start | bytes 1048576 | tf_op jit(solution)/shard_map/all_to_all | solution.py:175
  349.4 111.3 %all-gather.3.cloned.1.call-start = ((), (), s32[]{:S(2)}) async-start(), calls=%async_computation.7 | async-start | bytes 12582912 | tf_op jit(solution)/shard_map/all_gather | solution.py:197
  359.7 5.8 copy-start.16
  499.3 8.2 %copy-start.2 = (f32[2,64,16,2048]{3,2,1,0:T(8,128)}, f32[2,64,16,2048]{3,2,1,0:T(8,128)S(1)}, u32[]{:S(2)}) copy-start(f32[2,64,16,2048]{3,2,1,0:T(8,128)S(1)} %fusion.39) | copy-start | bytes 50331652
  507.5 13.5 %collective-permute-start = (f32[64,16,2048]{2,1,0:T(8,128)}, f32[64,16,2048]{2,1,0:T(8,128)}, u32[]{:S(2)}, u32[]{:S(2)}) collective-permute-start(f32[64,16,2048]{2,1,0:T(8,128)} %dynamic-slice_bitcast_fusion), channel_id=1, source_target_pairs={{0,1},{1,0},{2,3},{3,2},{4,5},{5,4},{6,7},{7,6},{8,9},{9,8},{10,11... | collective-permute-start | bytes 25165832 | tf_op jit(solution)/shard_map/ppermute | solution.py:202
  530.2 11.1 %copy-start.14 = (s32[768]{0:T(1024)S(1)}, s32[768]{0:T(1024)}, u32[]{:S(2)}) copy-start(s32[768]{0:T(1024)} %copy-done.13) | copy-start | bytes 9220
  530.2 11.3 %copy-start.12 = (s32[128,6]{0,1:T(8,128)S(1)}, s32[128,6]{0,1:T(8,128)}, u32[]{:S(2)}) copy-start(s32[128,6]{0,1:T(8,128)} %param.26) | copy-start | bytes 9220
  530.2 11.5 %copy-start.18 = (f32[128,6]{0,1:T(8,128)S(1)}, f32[128,6]{0,1:T(8,128)}, u32[]{:S(2)}) copy-start(f32[128,6]{0,1:T(8,128)} %param.27) | copy-start | bytes 9220
  530.2 68.0 %all-to-all-start.6 = ((bf16[64,16,2048]{2,1,0:T(8,128)(2,1)}), bf16[64,16,2048]{2,1,0:T(8,128)(2,1)}, u32[]{:S(2)}, u32[]{:S(2)}) async-start(bf16[64,16,2048]{2,1,0:T(8,128)(2,1)} %fusion.35), calls=%async_computation.6 | async-start | bytes 8388608 | tf_op jit(solution)/shard_map/all_to_all | solution.py:204
  614.3 6.1 copy-start.4
  (7 other events, 12.3 us)
Sparse Core Ops, SparseCore 0:
  439.0 21.6 all-gather.2
